TPU v7x, 128 devices: a whole 4x4x4 slice. The times are simulated.
128 devices in a mesh: prow: 16 (over y, x_hi, core), pcol: 8 (over x_lo, z).
Axes of the slice: x: 4 (x_hi: 2, x_lo: 2; x = x_hi * 2 + x_lo), y: 4, z: 4, core: 2. Of those that a mesh axis runs over, the one named last changes fastest.
Arguments:
- inverse_block: float32 [3, 16, 256, 6, 8, 256], P(None, 'prow', None, None, 'pcol'), as said below
- panel_first: float32 [3, 16, 256, 512], P(None, 'prow', 'pcol'), may hold values from -0.0546875 to 0.0546875
- panel_second: float32 [3, 16, 256, 512], P(None, 'prow', 'pcol'), may hold values from -0.0546875 to 0.0546875
- diag_first: float32 [512, 512], replicated, may hold values from -6 to 6
- diag_second: float32 [512, 512], replicated, may hold values from -6 to 6
- pattern_first: int32 [48], replicated, may hold values from 0 to 1, as said below
- pattern_second: int32 [48], replicated, may hold values from 0 to 1, as said below
Outputs:
- column_first: float32 [3, 16, 256, 512], P(None, 'prow', 'pcol')
- column_second: float32 [3, 16, 256, 512], P(None, 'prow', 'pcol')
- diagonal_first: float32 [512, 512], replicated
- diagonal_second: float32 [512, 512], replicated
Inputs may be any that keep to these rules, and one draw needn't show every extreme that they name: inverse_block is symmetric as a matrix of 12288 rows: its entry (i, j) equals its entry (j, i) exactly. `pattern_first`: at least one entry is 1. `pattern_second`: at least one entry is 1.
All inputs are finite; a program needn't handle non-finite values.
Results may differ from a plain program's by a relative error of at most 0.000071.
Values sent between devices are 32-bit elements; how exact they have to be, the bound alone decides.
No kernel may reach another device: no remote copies, remote signals or barrier semaphores. Data moves between devices by JAX's collectives and lax.ppermute only.
A program may use at most 64 MiB of HBM per device.

v0:
```python
import jax
import jax.numpy as jnp
from jax import lax
from jax.sharding import PartitionSpec as P


def from_root(block, axis, owner):
    block = jnp.where(lax.axis_index(axis) == owner, block, jnp.zeros_like(block))
    return lax.psum(block, axis)


def body(
    inverse_block, panel_first, panel_second, diag_first, diag_second, pattern_first, pattern_second
):
    row_count = lax.axis_size("prow")
    col_count = lax.axis_size("pcol")
    factor = row_count // col_count
    row_index = lax.axis_index("prow")
    col_index = lax.axis_index("pcol")
    row_blocks = inverse_block.shape[0]
    block_rows = inverse_block.shape[2]
    col_blocks = inverse_block.shape[3]
    matrix = inverse_block.reshape(row_blocks, block_rows, col_blocks, block_rows)
    slice_rows = panel_first.shape[2]
    col_width = panel_first.shape[3]
    highest = lax.Precision.HIGHEST

    def one_column(panel_part, pattern):
        kept_rows = lax.dynamic_index_in_dim(
            pattern.reshape(row_blocks, row_count), row_index, 1, False
        ).astype(jnp.float32)
        masked = panel_part[:, 0] * kept_rows[:, None, None]
        whole = lax.all_gather(masked, "pcol", axis=1, tiled=True)
        partial_value = jnp.einsum(
            "lsmt,lsw->mtw", matrix, whole, precision=highest, preferred_element_type=jnp.float32
        )
        totals = lax.psum(partial_value, "prow")
        chosen = lax.dynamic_index_in_dim(
            totals.reshape(row_blocks, factor, block_rows, col_width),
            row_index // col_count,
            1,
            False,
        )
        row_full = from_root(chosen, "pcol", row_index % col_count)
        result = -lax.dynamic_slice_in_dim(row_full, col_index * slice_rows, slice_rows, 1)
        result = result * kept_rows[:, None, None]
        partial_diag = jnp.einsum(
            "lsw,lsv->wv", masked, result, precision=highest, preferred_element_type=jnp.float32
        )
        return (result, partial_diag)

    first_col, first_part = one_column(panel_first, pattern_first)
    second_col, second_part = one_column(panel_second, pattern_second)
    first_sum, second_sum = lax.psum((first_part, second_part), ("prow", "pcol"))
    return (
        first_col[:, None],
        second_col[:, None],
        diag_first - first_sum,
        diag_second - second_sum,
    )


def solution(mesh):
    placed = (
        P(None, "prow", None, None, "pcol", None),
        P(None, "prow", "pcol", None),
        P(None, "prow", "pcol", None),
        P(),
        P(),
        P(),
        P(),
    )
    return jax.shard_map(
        body,
        mesh=mesh,
        in_specs=placed,
        out_specs=(P(None, "prow", "pcol", None), P(None, "prow", "pcol", None), P(), P()),
        check_vma=False,
    )
```

profile of v0, /device:TPU:6, one launch (start us, length us, event | category | flops | bytes accessed | tf_op | source)
XLA Modules:
  0.0 536.8 jit_solution(550724028770213054)
XLA Ops:
  7.2 0.7 reshape.41
  8.0 0.2 convert_reduce_fusion.1
  8.1 1.7 bitcast_multiply_fusion.1
  9.9 0.7 reshape.44
  10.6 0.2 convert_reduce_fusion
  10.8 1.7 bitcast_multiply_fusion
  12.5 0.0 all-reduce.9.cloned.1.call-start
  12.6 39.3 %all-gather.3.cloned.1.call-done = f32[3,256,512]{2,1,0:T(8,128)} async-done(((f32[3,32,512]{2,1,0:T(8,128)}), f32[3,256,512]{2,1,0:T(8,128)}) %all-gather.3.cloned.1.call-update) | async-done | bytes 1572880 | tf_op jit(solution)/shard_map/all_gather | solution.py:33
  51.9 10.4 %fusion.2 = f32[512,6,256,1]{2,0,3,1:T(8,128)S(1)} fusion(f32[3,1,256,6,1,256]{5,4,3,2,1,0:T(1,128)} %param.7, f32[3,256,512]{2,1,0:T(8,128)} %all-gather.3.cloned.1.call-done), kind=kOutput, calls=%fused_computation.2 | convolution fusion | flops 7247757312 | bytes 9437184 | tf_op jit(solution)/shard_map/lsmt,lsw->mtw/dot_general | solution.py:34
  62.3 2.4 copy.18
  64.8 29.0 %all-gather.5.cloned.1.call-done = f32[3,256,512]{2,1,0:T(8,128)} async-done(((f32[3,32,512]{2,1,0:T(8,128)}), f32[3,256,512]{2,1,0:T(8,128)}) %all-gather.5.cloned.1.call-update) | async-done | bytes 1572880 | tf_op jit(solution)/shard_map/all_gather | solution.py:33
  93.7 10.4 %fusion = f32[512,6,256,1]{2,0,3,1:T(8,128)S(1)} fusion(f32[3,1,256,6,1,256]{5,4,3,2,1,0:T(1,128)} %param.7, f32[3,256,512]{2,1,0:T(8,128)} %all-gather.5.cloned.1.call-done), kind=kOutput, calls=%fused_computation | convolution fusion | flops 7247757312 | bytes 9437184 | tf_op jit(solution)/shard_map/lsmt,lsw->mtw/dot_general | solution.py:34
  104.1 2.3 copy.21
  106.6 165.0 %all-reduce.9.cloned.1.call-done = (f32[3,2,256,512]{3,2,0,1:T(8,128)}, f32[3,2,256,512]{3,2,0,1:T(8,128)}) async-done(((f32[3,2,256,512]{3,2,0,1:T(8,128)}, f32[3,2,256,512]{3,2,0,1:T(8,128)}), (f32[3,2,256,512]{3,2,0,1:T(8,128)}, f32[3,2,256,512]{3,2,0,1:T(8,128)})) %all-reduce.9.cloned.1.call-update) | async-done | bytes 6291472 | tf_op jit(solution)/shard_map/psum | solution.py:37
  271.6 4.2 select_bitcast_fusion
  275.9 0.2 all-reduce.7.cloned.1.call-start
  276.1 93.6 %all-reduce.11.cloned.1.call-done = (f32[3,256,512]{2,1,0:T(8,128)}, f32[3,256,512]{2,1,0:T(8,128)}) async-done(((f32[3,256,512]{2,1,0:T(8,128)}, f32[3,256,512]{2,1,0:T(8,128)}), (f32[3,256,512]{2,1,0:T(8,128)}, f32[3,256,512]{2,1,0:T(8,128)})) %all-reduce.11.cloned.1.call-update) | async-done | bytes 3145744 | tf_op jit(solution)/shard_map/psum | solution.py:9
  369.7 3.0 convolution_bitcast_fusion.1
  372.7 3.0 convolution_bitcast_fusion
  375.7 1.8 fusion.8
  377.5 1.7 fusion.9
  379.2 147.3 %all-reduce.7.cloned.1.call-done = (f32[512,512]{1,0:T(8,128)}, f32[512,512]{1,0:T(8,128)}) async-done(((f32[512,512]{1,0:T(8,128)}, f32[512,512]{1,0:T(8,128)}), (f32[512,512]{1,0:T(8,128)}, f32[512,512]{1,0:T(8,128)})) %all-reduce.7.cloned.1.call-update) | async-done | bytes 2097168 | tf_op jit(solution)/shard_map/psum | solution.py:54
  526.5 2.5 sub.12
  529.1 1.2 sub.13
  (18 shorter events, 0.2 us)
Async XLA Ops:
  7.2 44.8 %all-gather.3.cloned.1.call-start = ((), (), s32[]{:S(2)}) async-start(), calls=%async_computation | async-start | bytes 1769472 | tf_op jit(solution)/shard_map/all_gather | solution.py:33
  9.9 83.9 %all-gather.5.cloned.1.call-start = ((), (), s32[]{:S(2)}) async-start(), calls=%async_computation.1 | async-start | bytes 1769472 | tf_op jit(solution)/shard_map/all_gather | solution.py:33
  12.5 259.1 %all-reduce.9.cloned.1.call-start = ((), (), s32[]{:S(2)}) async-start(), calls=%async_computation.3 | async-start | bytes 12582912 | tf_op jit(solution)/shard_map/psum | solution.py:37
  106.5 263.1 %all-reduce.11.cloned.1.call-start = ((), (), s32[]{:S(2)}) async-start(), calls=%async_computation.4 | async-start | bytes 6291456 | tf_op jit(solution)/shard_map/psum | solution.py:9
  275.8 93.8 %copy-start.3 = (f32[3,1,32,512]{3,2,1,0:T(8,128)S(1)}, f32[3,1,32,512]{3,2,1,0:T(8,128)}, u32[]{:S(2)}) copy-start(f32[3,1,32,512]{3,2,1,0:T(8,128)} %param.8) | copy-start | bytes 589828
  275.8 96.8 %copy-start.4 = (f32[3,1,32,512]{3,2,1,0:T(8,128)S(1)}, f32[3,1,32,512]{3,2,1,0:T(8,128)}, u32[]{:S(2)}) copy-start(f32[3,1,32,512]{3,2,1,0:T(8,128)} %param.9) | copy-start | bytes 589828
  275.9 250.6 %all-reduce.7.cloned.1.call-start = ((), (), s32[]{:S(2)}) async-start(), calls=%async_computation.2 | async-start | bytes 4194304 | tf_op jit(solution)/shard_map/psum | solution.py:54
  375.7 150.8 %copy-start = (f32[512,512]{1,0:T(8,128)S(1)}, f32[512,512]{1,0:T(8,128)}, u32[]{:S(2)}) copy-start(f32[512,512]{1,0:T(8,128)} %param.10) | copy-start | bytes 3145732
  526.5 2.6 copy-start.1
  526.5 2.6 copy-start.2
Sparse Core Ops, SparseCore 0:
  10.2 41.6 all-gather.2
  54.1 39.5 all-gather.4
  106.6 164.9 all-reduce.8
  276.0 93.6 all-reduce.10
  375.8 150.6 all-reduce.6
where the time goes:
time: 539 us; the launch traced here: 537 us
  waiting for transfers between devices  474 us (88%)
  matrix products  26.8 us (5%)
  other arithmetic  15.1 us (3%)
  between operations  13.8 us (3%)
  local copies, waits for them, and re-layouts  6.26 us (1%)
    psum x1, waiting for transfers between devices, one_column(): totals = lax.psum(partial_value, 'prow')  165 us
    psum x1, waiting for transfers between devices, body(): lax.psum((first_part, second_part), ('prow', 'pcol'))  147 us
    psum x1, waiting for transfers between devices, from_root(): return lax.psum(block, axis)  93.6 us
    all_gather x2, waiting for transfers between devices, one_column(): whole = lax.all_gather(masked, 'pcol', axis=1, tiled=True)  68.3 us
    dot_general x2, matrix products, one_column(): jnp.einsum('lsmt,lsw->mtw', matrix, whole, precision=highest, preferred_e...  20.8 us
  transfers between devices with their start and end apart: 5, of which 5 were waited for; matrix products, arithmetic and copies ran while one was open for 4% of the time, Pallas kernels for 0%

commit v1 on v0

v1 whole, which is shorter than its diff:
```python
import jax
import jax.numpy as jnp
from jax import lax
from jax.sharding import PartitionSpec as P

TILE = 128


def pack_upper(d):
    n = d.shape[-1] // TILE
    blocks = [
        d[..., i * TILE:(i + 1) * TILE, j * TILE:(j + 1) * TILE]
        for i in range(n)
        for j in range(i, n)
    ]
    return jnp.stack(blocks, axis=-3)


def unpack_upper(packed, n):
    rows = [[None] * n for _ in range(n)]
    k = 0
    for i in range(n):
        for j in range(i, n):
            blk = packed[..., k, :, :]
            rows[i][j] = blk
            if i != j:
                rows[j][i] = jnp.swapaxes(blk, -1, -2)
            k += 1
    return jnp.concatenate([jnp.concatenate(r, axis=-1) for r in rows], axis=-2)


def body(
    inverse_block, panel_first, panel_second, diag_first, diag_second, pattern_first, pattern_second
):
    row_count = lax.axis_size("prow")
    col_count = lax.axis_size("pcol")
    factor = row_count // col_count
    row_index = lax.axis_index("prow")
    col_index = lax.axis_index("pcol")
    row_blocks = inverse_block.shape[0]
    block_rows = inverse_block.shape[2]
    col_blocks = inverse_block.shape[3]
    slice_rows = panel_first.shape[2]
    width = panel_first.shape[3]
    highest = lax.Precision.HIGHEST
    both = ("prow", "pcol")

    def kept_of(pattern, prow):
        return lax.dynamic_index_in_dim(
            pattern.reshape(row_blocks, row_count), prow, 1, False
        ).astype(jnp.float32)

    own_first = kept_of(pattern_first, row_index)
    own_second = kept_of(pattern_second, row_index)
    x = jnp.concatenate(
        [
            panel_first[:, 0] * own_first[:, None, None],
            panel_second[:, 0] * own_second[:, None, None],
        ],
        axis=-1,
    )

    to_reducer = []
    to_owner = []
    for q in range(row_count):
        for c in range(col_count):
            reducer = (col_count * (q // col_count) + c) * col_count + q % col_count
            to_reducer.append((q * col_count + c, reducer))
            to_owner.append((reducer, q * col_count + c))
    x_at_reducer = lax.ppermute(x, both, to_reducer)

    spread = jnp.broadcast_to(x[None], (col_count,) + x.shape)
    gathered = lax.all_to_all(spread, "pcol", 0, 0, tiled=True)
    matrix = inverse_block.reshape(
        row_blocks, col_count, slice_rows, row_blocks, factor, col_count, slice_rows
    )
    partial = jnp.einsum(
        "ljsmpct,jlsw->pcmtw",
        matrix,
        gathered,
        precision=highest,
        preferred_element_type=jnp.float32,
    )
    chunks = partial.reshape(row_count, row_blocks, slice_rows, 2 * width)
    received = lax.all_to_all(chunks, "prow", 0, 0, tiled=True)
    total = jnp.sum(received, axis=0)

    owner_row = col_index + col_count * (row_index // col_count)
    kept_first = kept_of(pattern_first, owner_row)
    kept_second = kept_of(pattern_second, owner_row)
    column = jnp.concatenate(
        [
            -(total[..., :width] * kept_first[:, None, None]),
            -(total[..., width:] * kept_second[:, None, None]),
        ],
        axis=-1,
    )
    parts = jnp.stack(
        [
            jnp.einsum(
                "lsw,lsv->wv",
                x_at_reducer[..., :width],
                column[..., :width],
                precision=highest,
                preferred_element_type=jnp.float32,
            ),
            jnp.einsum(
                "lsw,lsv->wv",
                x_at_reducer[..., width:],
                column[..., width:],
                precision=highest,
                preferred_element_type=jnp.float32,
            ),
        ]
    )
    column_home = lax.ppermute(column, both, to_owner)
    sums = unpack_upper(lax.psum(pack_upper(parts), both), width // TILE)
    return (
        column_home[:, None, :, :width],
        column_home[:, None, :, width:],
        diag_first - sums[0],
        diag_second - sums[1],
    )


def solution(mesh):
    placed = (
        P(None, "prow", None, None, "pcol", None),
        P(None, "prow", "pcol", None),
        P(None, "prow", "pcol", None),
        P(),
        P(),
        P(),
        P(),
    )
    return jax.shard_map(
        body,
        mesh=mesh,
        in_specs=placed,
        out_specs=(P(None, "prow", "pcol", None), P(None, "prow", "pcol", None), P(), P()),
        check_vma=False,
    )
```

time: 539 us -> 377 us (0.70)
  waiting for transfers between devices: 474 us -> 228 us
  starting transfers between devices: 0.39 us -> 24 us
  other arithmetic: 15.1 us -> 36.3 us
  local copies, waits for them, and re-layouts: 6.26 us -> 26.1 us
  matrix products: 26.8 us -> 46.1 us
    psum x3 -> x1, waiting for transfers between devices: 406 us -> 134 us  [body(): sums = unpack_upper(lax.psum(pack_upper(parts), both), width // TILE)]
    all_gather x2 -> x0, waiting for transfers between devices: 68.3 us -> none  [one_column(): whole = lax.all_gather(masked, 'pcol', axis=1, tiled=True)]
    all_to_all x0 -> x2, waiting for transfers between devices: none -> 65.9 us  [the longest x1 65.9 us: body(): received = lax.all_to_all(chunks, 'prow', 0, 0, tiled=True)]
    ppermute x0 -> x2, waiting for transfers between devices: none -> 28 us  [the longest x1 14.3 us: body(): x_at_reducer = lax.ppermute(x, both, to_reducer)]
    unnamed x2 -> x10, other arithmetic: 3.46 us -> 28.5 us
    dot_general x4 -> x3, matrix products: 26.8 us -> 46.1 us  [the longest x1 44 us: body(): jnp.einsum('ljsmpct,jlsw->pcmtw', matrix, gathered, precision=highest, pr...]
    all_to_all x0 -> x2, starting transfers between devices: none -> 14.2 us  [the longest x1 7.44 us: body(): received = lax.all_to_all(chunks, 'prow', 0, 0, tiled=True)]
    reshape x4, local copies, waits for them, and re-layouts: 6.25 us -> 18.4 us  [the longest x1 13.2 us: body(): inverse_block.reshape(row_blocks, col_count, slice_rows, row_blocks, fact...]
  transfers between devices with their start and end apart: 5 -> 5, of which waited for: 5 -> 4; matrix products, arithmetic and copies ran while one was open for 4% -> 12% of each run, Pallas kernels for 0% -> 0%
where the time goes in v1:
time: 377 us; the launch traced here: 375 us
  waiting for transfers between devices  228 us (60%)
  matrix products  46.1 us (12%)
  other arithmetic  36.3 us (10%)
  local copies, waits for them, and re-layouts  26.1 us (7%)
  starting transfers between devices  24 us (6%)
  between operations  14.3 us (4%)
    psum x1, waiting for transfers between devices, body(): sums = unpack_upper(lax.psum(pack_upper(parts), both), width // TILE)  134 us
    all_to_all x1, waiting for transfers between devices, body(): received = lax.all_to_all(chunks, 'prow', 0, 0, tiled=True)  65.9 us
    dot_general x1, matrix products, body(): jnp.einsum('ljsmpct,jlsw->pcmtw', matrix, gathered, precision=highest, pr...  44 us
    unnamed x10, other arithmetic  28.5 us
    ppermute x1, waiting for transfers between devices, body(): x_at_reducer = lax.ppermute(x, both, to_reducer)  14.3 us
    ppermute x1, waiting for transfers between devices, body(): column_home = lax.ppermute(column, both, to_owner)  13.6 us
    reshape x1, local copies, waits for them, and re-layouts, body(): inverse_block.reshape(row_blocks, col_count, slice_rows, row_blocks, fact...  13.2 us
  transfers between devices with their start and end apart: 5, of which 4 were waited for; matrix products, arithmetic and copies ran while one was open for 12% of the time, Pallas kernels for 0%

profile of v1, /device:TPU:6, one launch (start us, length us, event | category | flops | bytes accessed | tf_op | source)
XLA Modules:
  0.0 374.8 jit_solution(4883474048962763448)
XLA Ops:
  7.2 0.7 reshape.47
  8.9 1.0 bitcast_multiply_fusion
  9.9 1.0 bitcast_multiply_fusion.1
  10.9 2.2 broadcast_in_dim.6
  13.1 6.8 %all-to-all-start = ((f32[8,3,32,1024]{3,2,1,0:T(8,128)}), f32[8,3,32,1024]{3,2,1,0:T(8,128)S(1)}, u32[]{:S(2)}, u32[]{:S(2)}) async-start(f32[8,3,32,1024]{3,2,1,0:T(8,128)} %broadcast_in_dim.6), calls=%async_computation | async-start | bytes 6291456 | tf_op jit(solution)/shard_map/all_to_all | solution.py:73
  19.9 28.3 %reduce.2 = f32[3,256,6,256]{3,2,1,0:T(8,128)} reduce(f32[3,1,256,6,1,256]{5,4,3,2,1,0:T(1,128)} %param.7, f32[]{:T(128)} %constant.42), dimensions={1,4}, to_apply=%param.7.reduce_sub_computation | reduce | bytes 9437188 | tf_op args[0]
  48.2 13.2 %reshape.49 = f32[3,8,32,3,2,8,32]{6,5,4,3,2,1,0:T(8,128)} reshape(f32[3,256,6,256]{3,2,1,0:T(8,128)} %reduce.2) | data formatting | bytes 9437184 | tf_op jit(solution)/shard_map/reshape | solution.py:74
  61.4 44.0 %fusion = f32[1024,3,2,8,32,1,1]{0,4,6,5,3,2,1:T(8,128)S(1)} fusion(f32[3,8,32,3,2,8,32]{6,5,4,3,2,1,0:T(8,128)} %reshape.49, f32[8,3,32,1024]{3,2,1,0:T(8,128)S(1)} %all-to-all-done), kind=kOutput, calls=%fused_computation | convolution fusion | flops 14495514624 | bytes 14155776 | tf_op jit(solution)/shard_map/ljsmpct,jlsw->pcmtw/dot_general | solution.py:77
  105.4 3.8 %copy.28 = f32[16,3,32,1024]{3,2,1,0:T(8,128)} copy(f32[16,3,32,1024]{3,2,0,1:T(8,128)S(1)} %bitcast.110) | data formatting | bytes 12582912 | tf_op jit(solution)/shard_map/reshape | solution.py:84
  109.2 7.4 %all-to-all-start.1 = ((f32[16,3,32,1024]{3,2,1,0:T(8,128)}), f32[16,3,32,1024]{3,2,1,0:T(8,128)}, u32[]{:S(2)}, u32[]{:S(2)}) async-start(f32[16,3,32,1024]{3,2,1,0:T(8,128)} %copy.28), calls=%async_computation.1 | async-start | bytes 12582912 | tf_op jit(solution)/shard_map/all_to_all | solution.py:85
  116.7 5.7 %collective-permute-start.1 = (f32[3,32,1024]{2,1,0:T(8,128)S(1)}, f32[3,32,1024]{2,1,0:T(8,128)S(1)}, u32[]{:S(2)}, u32[]{:S(2)}) collective-permute-start(f32[3,32,1024]{2,1,0:T(8,128)S(1)} %pad_maximum_fusion.1), channel_id=1, source_target_pairs={{0,0},{1,8},{2,16},{3,24},{4,32},{5,40},{6,48},{7,56},{8,1},{9,9},... | collective-permute-start | bytes 1179656 | tf_op jit(solution)/shard_map/ppermute | solution.py:70
  122.4 65.9 %all-to-all-done.1 = f32[16,3,32,1024]{3,2,1,0:T(8,128)} async-done(((f32[16,3,32,1024]{3,2,1,0:T(8,128)}), f32[16,3,32,1024]{3,2,1,0:T(8,128)}, u32[]{:S(2)}, u32[]{:S(2)}) %all-to-all-start.1) | async-done | bytes 6291488 | tf_op jit(solution)/shard_map/all_to_all | solution.py:85
  188.3 3.4 reduce_sum.9
  191.8 14.3 %collective-permute-done.1 = f32[3,32,1024]{2,1,0:T(8,128)S(1)} collective-permute-done((f32[3,32,1024]{2,1,0:T(8,128)S(1)}, f32[3,32,1024]{2,1,0:T(8,128)S(1)}, u32[]{:S(2)}, u32[]{:S(2)}) %collective-permute-start.1) | collective-permute-done | bytes 393248 | tf_op jit(solution)/shard_map/ppermute | solution.py:70
  206.1 1.0 convolution_bitcast_fusion.1
  207.1 1.0 convolution_bitcast_fusion
  208.4 1.1 copy-done
  209.6 4.0 %collective-permute-start = (f32[3,32,1024]{2,1,0:T(8,128)S(1)}, f32[3,32,1024]{2,1,0:T(8,128)S(1)}, u32[]{:S(2)}, u32[]{:S(2)}) collective-permute-start(f32[3,32,1024]{2,1,0:T(8,128)S(1)} %pad_maximum_fusion.2), channel_id=1, source_target_pairs={{0,0},{8,1},{16,2},{24,3},{32,4},{40,5},{48,6},{56,7},{1,8},{9,9},... | collective-permute-start | bytes 1179656 | tf_op jit(solution)/shard_map/ppermute | solution.py:116
  213.6 13.6 %collective-permute-done = f32[3,32,1024]{2,1,0:T(8,128)S(1)} collective-permute-done((f32[3,32,1024]{2,1,0:T(8,128)S(1)}, f32[3,32,1024]{2,1,0:T(8,128)S(1)}, u32[]{:S(2)}, u32[]{:S(2)}) %collective-permute-start) | collective-permute-done | bytes 393248 | tf_op jit(solution)/shard_map/ppermute | solution.py:116
  227.2 0.8 slice_bitcast_fusion.2
  228.0 134.2 %all-reduce.2.cloned.1.call-done = f32[2,10,128,128]{3,2,0,1:T(8,128)} async-done(((f32[2,10,128,128]{3,2,0,1:T(8,128)}), f32[2,10,128,128]{3,2,0,1:T(8,128)}) %all-reduce.2.cloned.1.call-update) | async-done | bytes 1310736 | tf_op jit(solution)/shard_map/psum | solution.py:117
  362.2 1.6 slice_bitcast_fusion.6
  364.9 1.0 copy-done.1
  366.2 1.8 fusion.3
  (31 shorter events, 2.7 us)
Async XLA Ops:
  13.1 48.3 %all-to-all-start = ((f32[8,3,32,1024]{3,2,1,0:T(8,128)}), f32[8,3,32,1024]{3,2,1,0:T(8,128)S(1)}, u32[]{:S(2)}, u32[]{:S(2)}) async-start(f32[8,3,32,1024]{3,2,1,0:T(8,128)} %broadcast_in_dim.6), calls=%async_computation | async-start | bytes 6291456 | tf_op jit(solution)/shard_map/all_to_all | solution.py:73
  109.2 79.1 %all-to-all-start.1 = ((f32[16,3,32,1024]{3,2,1,0:T(8,128)}), f32[16,3,32,1024]{3,2,1,0:T(8,128)}, u32[]{:S(2)}, u32[]{:S(2)}) async-start(f32[16,3,32,1024]{3,2,1,0:T(8,128)} %copy.28), calls=%async_computation.1 | async-start | bytes 12582912 | tf_op jit(solution)/shard_map/all_to_all | solution.py:85
  116.7 245.5 %all-reduce.2.cloned.1.call-start = ((), (), s32[]{:S(2)}) async-start(), calls=%async_computation.2 | async-start | bytes 2621440 | tf_op jit(solution)/shard_map/psum | solution.py:117
  116.7 89.4 %collective-permute-start.1 = (f32[3,32,1024]{2,1,0:T(8,128)S(1)}, f32[3,32,1024]{2,1,0:T(8,128)S(1)}, u32[]{:S(2)}, u32[]{:S(2)}) collective-permute-start(f32[3,32,1024]{2,1,0:T(8,128)S(1)} %pad_maximum_fusion.1), channel_id=1, source_target_pairs={{0,0},{1,8},{2,16},{3,24},{4,32},{5,40},{6,48},{7,56},{8,1},{9,9},... | collective-permute-start | bytes 1179656 | tf_op jit(solution)/shard_map/ppermute | solution.py:70
  208.4 1.1 copy-start
  209.6 17.7 %collective-permute-start = (f32[3,32,1024]{2,1,0:T(8,128)S(1)}, f32[3,32,1024]{2,1,0:T(8,128)S(1)}, u32[]{:S(2)}, u32[]{:S(2)}) collective-permute-start(f32[3,32,1024]{2,1,0:T(8,128)S(1)} %pad_maximum_fusion.2), channel_id=1, source_target_pairs={{0,0},{8,1},{16,2},{24,3},{32,4},{40,5},{48,6},{56,7},{1,8},{9,9},... | collective-permute-start | bytes 1179656 | tf_op jit(solution)/shard_map/ppermute | solution.py:116
  364.6 1.2 copy-start.1
  364.6 1.5 copy-start.2
Sparse Core Ops, SparseCore 0:
  209.7 152.4 all-reduce.1

commit v2 on v1

--- a/solution.py
+++ b/solution.py
@@ -69,21 +69,21 @@
             to_owner.append((reducer, q * col_count + c))
     x_at_reducer = lax.ppermute(x, both, to_reducer)
 
-    spread = jnp.broadcast_to(x[None], (col_count,) + x.shape)
-    gathered = lax.all_to_all(spread, "pcol", 0, 0, tiled=True)
-    matrix = inverse_block.reshape(
-        row_blocks, col_count, slice_rows, row_blocks, factor, col_count, slice_rows
-    )
+    spread = jnp.broadcast_to(
+        x[:, None], (row_blocks, col_count, slice_rows, 2 * width)
+    ).reshape(row_blocks, block_rows, 2 * width)
+    gathered = lax.all_to_all(spread, "pcol", 1, 1, tiled=True)
+    matrix = inverse_block.reshape(row_blocks, block_rows, col_blocks, block_rows)
     partial = jnp.einsum(
-        "ljsmpct,jlsw->pcmtw",
+        "lsmt,lsw->mtw",
         matrix,
         gathered,
         precision=highest,
         preferred_element_type=jnp.float32,
     )
-    chunks = partial.reshape(row_count, row_blocks, slice_rows, 2 * width)
-    received = lax.all_to_all(chunks, "prow", 0, 0, tiled=True)
-    total = jnp.sum(received, axis=0)
+    chunks = partial.reshape(row_blocks, row_count, slice_rows, 2 * width)
+    received = lax.all_to_all(chunks, "prow", 1, 1, tiled=True)
+    total = jnp.sum(received, axis=1)
 
     owner_row = col_index + col_count * (row_index // col_count)
     kept_first = kept_of(pattern_first, owner_row)
@@ -114,7 +114,13 @@
         ]
     )
     column_home = lax.ppermute(column, both, to_owner)
-    sums = unpack_upper(lax.psum(pack_upper(parts), both), width // TILE)
+    devices = row_count * col_count
+    packed = pack_upper(parts)
+    flat = packed.reshape(devices, packed.size // devices)
+    reduced = jnp.sum(lax.all_to_all(flat, both, 0, 0, tiled=True), axis=0)
+    spread_sum = jnp.broadcast_to(reduced[None], flat.shape)
+    summed = lax.all_to_all(spread_sum, both, 0, 0, tiled=True).reshape(packed.shape)
+    sums = unpack_upper(summed, width // TILE)
     return (
         column_home[:, None, :, :width],
         column_home[:, None, :, width:],

time: 377 us -> 259 us (0.69)
  waiting for transfers between devices: 228 us -> 110 us
  blocking collectives: 0 us -> 82.9 us
  other arithmetic: 36.3 us -> 8.74 us
  matrix products: 46.1 us -> 19.8 us
  local copies, waits for them, and re-layouts: 26.1 us -> 11 us
  between operations: 14.3 us -> 0.95 us
    psum x1 -> x0, waiting for transfers between devices: 134 us -> none  [body(): sums = unpack_upper(lax.psum(pack_upper(parts), both), width // TILE)]
    all_to_all x0 -> x2, blocking collectives: none -> 82.9 us  [the longest x1 55.2 us: body(): gathered = lax.all_to_all(spread, 'pcol', 1, 1, tiled=True)]
    unnamed x10, other arithmetic: 28.5 us -> 0.18 us
    dot_general x1, matrix products: 44 us -> 17.8 us  [body(): jnp.einsum('lsmt,lsw->mtw', matrix, gathered, precision=highest, preferre...]
    ppermute x1, waiting for transfers between devices: 13.6 us -> 29.8 us  [body(): column_home = lax.ppermute(column, both, to_owner)]
    reshape x2 -> x1, local copies, waits for them, and re-layouts: 17 us -> 3.23 us  [body(): chunks = partial.reshape(row_blocks, row_count, slice_rows, 2 * width)]
  transfers between devices with their start and end apart: 5 -> 4, of which waited for: 4 -> 3; matrix products, arithmetic and copies ran while one was open for 12% -> 2% of each run, Pallas kernels for 0% -> 0%
where the time goes in v2:
time: 259 us
  waiting for transfers between devices  110 us (42%)
  blocking collectives  82.9 us (32%)
  starting transfers between devices  25 us (10%)
  matrix products  19.8 us (8%)
  local copies, waits for them, and re-layouts  11 us (4%)
  other arithmetic  8.74 us (3%)
    all_to_all x1, waiting for transfers between devices, body(): received = lax.all_to_all(chunks, 'prow', 1, 1, tiled=True)  67.4 us
    all_to_all x1, blocking collectives, body(): gathered = lax.all_to_all(spread, 'pcol', 1, 1, tiled=True)  55.2 us
    ppermute x1, waiting for transfers between devices, body(): column_home = lax.ppermute(column, both, to_owner)  29.8 us
    all_to_all x1, blocking collectives, body(): reduced = jnp.sum(lax.all_to_all(flat, both, 0, 0, tiled=True), axis=0)  27.7 us
    dot_general x1, matrix products, body(): jnp.einsum('lsmt,lsw->mtw', matrix, gathered, precision=highest, preferre...  17.8 us
    ppermute x1, waiting for transfers between devices, body(): x_at_reducer = lax.ppermute(x, both, to_reducer)  13 us
    all_to_all x1, starting transfers between devices, body(): received = lax.all_to_all(chunks, 'prow', 1, 1, tiled=True)  7.44 us
    all_to_all x1, starting transfers between devices, body(): lax.all_to_all(spread_sum, both, 0, 0, tiled=True).reshape(packed.shape)  6.96 us
  transfers between devices with their start and end apart: 4, of which 3 were waited for; matrix products, arithmetic and copies ran while one was open for 2% of the time, Pallas kernels for 0%

profile of v2, /device:TPU:6, one launch (start us, length us, event | category | flops | bytes accessed | tf_op | source)
XLA Modules:
  0.0 258.6 jit_solution(6743640668196441663)
XLA Ops:
  0.6 0.7 reshape.64
  1.4 0.7 reshape.65
  2.3 1.0 bitcast_multiply_fusion
  3.4 1.0 bitcast_multiply_fusion.1
  4.7 1.1 broadcast_in_dim.8
  5.8 55.2 %all_to_all.25 = f32[3,256,1024]{2,0,1:T(4,128)S(1)} all-to-all(f32[3,256,1024]{2,0,1:T(4,128)S(1)} %bitcast.130), channel_id=1, replica_groups=mesh['prow'=16,'pcol'=8] {'pcol'}, dimensions={1} | all-to-all | bytes 6291456 | tf_op jit(solution)/shard_map/all_to_all | solution.py:75
  61.0 17.8 %fusion = f32[1024,6,256,1]{0,2,3,1:T(8,128)S(1)} fusion(f32[3,1,256,6,1,256]{5,4,3,2,1,0:T(1,128)S(1)} %bitcast.140, f32[3,256,1024]{2,0,1:T(4,128)S(1)} %all_to_all.25), kind=kOutput, calls=%fused_computation | convolution fusion | flops 14495514624 | bytes 14155776 | tf_op jit(solution)/shard_map/lsmt,lsw->mtw/dot_general | solution.py:77
  78.8 3.2 %copy.39 = f32[3,16,32,1024]{3,2,0,1:T(8,128)} copy(f32[3,16,32,1024]{3,2,1,0:T(8,128)S(1)} %bitcast.131) | data formatting | bytes 12582912 | tf_op jit(solution)/shard_map/reshape | solution.py:84
  82.1 7.4 %all-to-all-start.1 = ((f32[3,16,32,1024]{3,2,0,1:T(8,128)}), f32[3,16,32,1024]{3,2,0,1:T(8,128)}, u32[]{:S(2)}, u32[]{:S(2)}) async-start(f32[3,16,32,1024]{3,2,0,1:T(8,128)} %copy.39), calls=%async_computation.1 | async-start | bytes 12582912 | tf_op jit(solution)/shard_map/all_to_all | solution.py:85
  89.5 4.3 %collective-permute-start.1 = (f32[3,32,1024]{2,1,0:T(8,128)S(1)}, f32[3,32,1024]{2,1,0:T(8,128)S(1)}, u32[]{:S(2)}, u32[]{:S(2)}) collective-permute-start(f32[3,32,1024]{2,1,0:T(8,128)S(1)} %pad_maximum_fusion.1), channel_id=1, source_target_pairs={{0,0},{1,8},{2,16},{3,24},{4,32},{5,40},{6,48},{7,56},{8,1},{9,9},... | collective-permute-start | bytes 1179656 | tf_op jit(solution)/shard_map/ppermute | solution.py:70
  93.8 67.4 %all-to-all-done.1 = f32[3,16,32,1024]{3,2,0,1:T(8,128)} async-done(((f32[3,16,32,1024]{3,2,0,1:T(8,128)}), f32[3,16,32,1024]{3,2,0,1:T(8,128)}, u32[]{:S(2)}, u32[]{:S(2)}) %all-to-all-start.1) | async-done | bytes 6291488 | tf_op jit(solution)/shard_map/all_to_all | solution.py:85
  161.2 3.4 %reduce_sum.18 = f32[3,32,1024]{2,1,0:T(8,128)S(1)} reduce(f32[3,16,32,1024]{3,2,0,1:T(8,128)} %all-to-all-done.1, f32[]{:T(128)} %constant.32.clone.1), dimensions={1}, to_apply=%region_0.1 | reduce | flops 1474560 | bytes 6684676 | tf_op jit(solution)/shard_map/reduce_sum | solution.py:86
  164.6 13.0 %collective-permute-done.1 = f32[3,32,1024]{2,1,0:T(8,128)S(1)} collective-permute-done((f32[3,32,1024]{2,1,0:T(8,128)S(1)}, f32[3,32,1024]{2,1,0:T(8,128)S(1)}, u32[]{:S(2)}, u32[]{:S(2)}) %collective-permute-start.1) | collective-permute-done | bytes 393248 | tf_op jit(solution)/shard_map/ppermute | solution.py:70
  177.7 1.0 convolution_bitcast_fusion.1
  178.7 1.0 convolution_bitcast_fusion
  180.1 27.7 %all_to_all.26 = f32[128,1,2560]{2,1,0:T(1,128)S(1)} all-to-all(f32[128,1,2560]{2,1,0:T(1,128)S(1)} %bitcast.133), channel_id=1, replica_groups=mesh['prow'=16,'pcol'=8] {'prow','pcol'}, dimensions={0} | all-to-all | bytes 2621440 | tf_op jit(solution)/shard_map/all_to_all | solution.py:120
  207.8 0.8 reduce_sum.19
  208.5 1.7 broadcast_in_dim.11
  210.3 7.0 %all-to-all-start.3 = ((f32[128,1,2560]{2,1,0:T(1,128)}), f32[128,1,2560]{2,1,0:T(1,128)S(1)}, u32[]{:S(2)}, u32[]{:S(2)}) async-start(f32[128,1,2560]{2,1,0:T(1,128)} %broadcast_in_dim.11), calls=%async_computation.3 | async-start | bytes 2621440 | tf_op jit(solution)/shard_map/all_to_all | solution.py:122
  217.3 6.3 %collective-permute-start = (f32[3,32,1024]{2,1,0:T(8,128)S(1)}, f32[3,32,1024]{2,1,0:T(8,128)S(1)}, u32[]{:S(2)}, u32[]{:S(2)}) collective-permute-start(f32[3,32,1024]{2,1,0:T(8,128)S(1)} %pad_maximum_fusion.2), channel_id=1, source_target_pairs={{0,0},{8,1},{16,2},{24,3},{32,4},{40,5},{48,6},{56,7},{1,8},{9,9},... | collective-permute-start | bytes 1179656 | tf_op jit(solution)/shard_map/ppermute | solution.py:116
  223.6 29.8 %collective-permute-done = f32[3,32,1024]{2,1,0:T(8,128)S(1)} collective-permute-done((f32[3,32,1024]{2,1,0:T(8,128)S(1)}, f32[3,32,1024]{2,1,0:T(8,128)S(1)}, u32[]{:S(2)}, u32[]{:S(2)}) %collective-permute-start) | collective-permute-done | bytes 393248 | tf_op jit(solution)/shard_map/ppermute | solution.py:116
  253.4 0.8 slice_bitcast_fusion.2
  255.5 1.0 copy-done
  256.8 1.8 fusion.5
  (35 shorter events, 2.5 us)
Async XLA Ops:
  4.7 56.3 %slice-start = ((s8[4718592]{0:T(1024)(128)(4,1)}), s8[4194304]{0:T(1024)(128)(4,1)S(1)}, s32[]{:S(2)}) async-start(s8[4718592]{0:T(1024)(128)(4,1)} %bitcast.139), calls=%async_computation.4 | async-start | bytes 8388608
  5.8 55.3 %slice-start.1 = ((s8[4718592]{0:T(1024)(128)(4,1)}), s8[524288]{0:T(1024)(128)(4,1)S(1)}, s32[]{:S(2)}) async-start(s8[4718592]{0:T(1024)(128)(4,1)} %bitcast.139), calls=%async_computation.5 | async-start | bytes 1048576
  82.1 79.1 %all-to-all-start.1 = ((f32[3,16,32,1024]{3,2,0,1:T(8,128)}), f32[3,16,32,1024]{3,2,0,1:T(8,128)}, u32[]{:S(2)}, u32[]{:S(2)}) async-start(f32[3,16,32,1024]{3,2,0,1:T(8,128)} %copy.39), calls=%async_computation.1 | async-start | bytes 12582912 | tf_op jit(solution)/shard_map/all_to_all | solution.py:85
  89.5 88.2 %collective-permute-start.1 = (f32[3,32,1024]{2,1,0:T(8,128)S(1)}, f32[3,32,1024]{2,1,0:T(8,128)S(1)}, u32[]{:S(2)}, u32[]{:S(2)}) collective-permute-start(f32[3,32,1024]{2,1,0:T(8,128)S(1)} %pad_maximum_fusion.1), channel_id=1, source_target_pairs={{0,0},{1,8},{2,16},{3,24},{4,32},{5,40},{6,48},{7,56},{8,1},{9,9},... | collective-permute-start | bytes 1179656 | tf_op jit(solution)/shard_map/ppermute | solution.py:70
  210.3 43.9 %all-to-all-start.3 = ((f32[128,1,2560]{2,1,0:T(1,128)}), f32[128,1,2560]{2,1,0:T(1,128)S(1)}, u32[]{:S(2)}, u32[]{:S(2)}) async-start(f32[128,1,2560]{2,1,0:T(1,128)} %broadcast_in_dim.11), calls=%async_computation.3 | async-start | bytes 2621440 | tf_op jit(solution)/shard_map/all_to_all | solution.py:122
  217.3 36.1 %collective-permute-start = (f32[3,32,1024]{2,1,0:T(8,128)S(1)}, f32[3,32,1024]{2,1,0:T(8,128)S(1)}, u32[]{:S(2)}, u32[]{:S(2)}) collective-permute-start(f32[3,32,1024]{2,1,0:T(8,128)S(1)} %pad_maximum_fusion.2), channel_id=1, source_target_pairs={{0,0},{8,1},{16,2},{24,3},{32,4},{40,5},{48,6},{56,7},{1,8},{9,9},... | collective-permute-start | bytes 1179656 | tf_op jit(solution)/shard_map/ppermute | solution.py:116
  255.3 1.2 copy-start
  255.3 1.5 copy-start.1

commit v3 on v2

--- a/solution.py
+++ b/solution.py
@@ -4,6 +4,7 @@
 from jax.sharding import PartitionSpec as P
 
 TILE = 128
+PIECE = 512
 
 
 def pack_upper(d):
@@ -69,21 +70,28 @@
             to_owner.append((reducer, q * col_count + c))
     x_at_reducer = lax.ppermute(x, both, to_reducer)
 
-    spread = jnp.broadcast_to(
-        x[:, None], (row_blocks, col_count, slice_rows, 2 * width)
-    ).reshape(row_blocks, block_rows, 2 * width)
-    gathered = lax.all_to_all(spread, "pcol", 1, 1, tiled=True)
     matrix = inverse_block.reshape(row_blocks, block_rows, col_blocks, block_rows)
-    partial = jnp.einsum(
-        "lsmt,lsw->mtw",
-        matrix,
-        gathered,
-        precision=highest,
-        preferred_element_type=jnp.float32,
+
+    def reduce_piece(piece):
+        spread = jnp.broadcast_to(
+            piece[:, None], (row_blocks, col_count) + piece.shape[1:]
+        ).reshape(row_blocks, block_rows, piece.shape[-1])
+        gathered = lax.all_to_all(spread, "pcol", 1, 1, tiled=True)
+        partial = jnp.einsum(
+            "lsmt,lsw->mtw",
+            matrix,
+            gathered,
+            precision=highest,
+            preferred_element_type=jnp.float32,
+        )
+        chunks = partial.reshape(row_blocks, row_count, slice_rows, piece.shape[-1])
+        received = lax.all_to_all(chunks, "prow", 1, 1, tiled=True)
+        return jnp.sum(received, axis=1)
+
+    total = jnp.concatenate(
+        [reduce_piece(x[..., k * PIECE:(k + 1) * PIECE]) for k in range(2 * width // PIECE)],
+        axis=-1,
     )
-    chunks = partial.reshape(row_blocks, row_count, slice_rows, 2 * width)
-    received = lax.all_to_all(chunks, "prow", 1, 1, tiled=True)
-    total = jnp.sum(received, axis=1)
 
     owner_row = col_index + col_count * (row_index // col_count)
     kept_first = kept_of(pattern_first, owner_row)

time: 259 us -> 260 us (level)
  blocking collectives: 82.9 us -> 26.9 us
  waiting for transfers between devices: 110 us -> 140 us
  starting transfers between devices: 25 us -> 44 us
  matrix products: 19.8 us -> 25.3 us
  local copies, waits for them, and re-layouts: 11 us -> 14.2 us
    all_to_all x1 -> x0, blocking collectives: 55.2 us -> none  [body(): gathered = lax.all_to_all(spread, 'pcol', 1, 1, tiled=True)]
    all_to_all x1 -> x4, waiting for transfers between devices: 67.4 us -> 95.5 us  [the longest x2 56.9 us: reduce_piece(): received = lax.all_to_all(chunks, 'prow', 1, 1, tiled=True)]
    all_to_all x1 -> x4, starting transfers between devices: 7.44 us -> 26.2 us  [the longest x2 14.4 us: reduce_piece(): received = lax.all_to_all(chunks, 'prow', 1, 1, tiled=True)]
    dot_general x1 -> x2, matrix products: 17.8 us -> 21.4 us  [reduce_piece(): jnp.einsum('lsmt,lsw->mtw', matrix, gathered, precision=highest, preferre...]
    broadcast_in_dim x1 -> x4, local copies, waits for them, and re-layouts: 1.06 us -> 3.71 us  [reduce_piece(): jnp.broadcast_to(piece[:, None], (row_blocks, col_count) + piece.shape[1:])]
  transfers between devices with their start and end apart: 4 -> 7, of which waited for: 3 -> 6; matrix products, arithmetic and copies ran while one was open for 2% -> 12% of each run, Pallas kernels for 0% -> 0%
where the time goes in v3:
time: 260 us; the launch traced here: 259 us
  waiting for transfers between devices  140 us (54%)
  starting transfers between devices  44 us (17%)
  blocking collectives  26.9 us (10%)
  matrix products  25.3 us (10%)
  local copies, waits for them, and re-layouts  14.2 us (5%)
  other arithmetic  7.93 us (3%)
    all_to_all x2, waiting for transfers between devices, reduce_piece(): received = lax.all_to_all(chunks, 'prow', 1, 1, tiled=True)  56.9 us
    all_to_all x2, waiting for transfers between devices, reduce_piece(): gathered = lax.all_to_all(spread, 'pcol', 1, 1, tiled=True)  38.6 us
    ppermute x1, waiting for transfers between devices, body(): column_home = lax.ppermute(column, both, to_owner)  29.8 us
    all_to_all x1, blocking collectives, body(): reduced = jnp.sum(lax.all_to_all(flat, both, 0, 0, tiled=True), axis=0)  26.9 us
    dot_general x2, matrix products, reduce_piece(): jnp.einsum('lsmt,lsw->mtw', matrix, gathered, precision=highest, preferre...  21.4 us
    all_to_all x2, starting transfers between devices, reduce_piece(): received = lax.all_to_all(chunks, 'prow', 1, 1, tiled=True)  14.4 us
    ppermute x1, waiting for transfers between devices, body(): x_at_reducer = lax.ppermute(x, both, to_reducer)  14.3 us
    all_to_all x2, starting transfers between devices, reduce_piece(): gathered = lax.all_to_all(spread, 'pcol', 1, 1, tiled=True)  11.7 us
  transfers between devices with their start and end apart: 7, of which 6 were waited for; matrix products, arithmetic and copies ran while one was open for 12% of the time, Pallas kernels for 0%

profile of v3, /device:TPU:6, one launch (start us, length us, event | category | flops | bytes accessed | tf_op | source)
XLA Modules:
  0.0 258.9 jit_solution(9807108336938573072)
XLA Ops:
  5.2 6.9 %all-to-all-start.2 = ((f32[3,256,512]{2,0,1:T(4,128)}), f32[3,256,512]{2,0,1:T(4,128)S(1)}, u32[]{:S(2)}, u32[]{:S(2)}) async-start(f32[3,256,512]{2,0,1:T(4,128)} %bitcast.11), calls=%async_computation.2 | async-start | bytes 4194304 | tf_op jit(solution)/shard_map/all_to_all | solution.py:79
  12.4 25.2 %all-to-all-done.2 = f32[3,256,512]{2,0,1:T(4,128)S(1)} async-done(((f32[3,256,512]{2,0,1:T(4,128)}), f32[3,256,512]{2,0,1:T(4,128)S(1)}, u32[]{:S(2)}, u32[]{:S(2)}) %all-to-all-start.2) | async-done | bytes 1572896 | tf_op jit(solution)/shard_map/all_to_all | solution.py:79
  37.6 1.7 broadcast_in_dim.15
  39.3 4.8 %all-to-all-start = ((f32[3,256,512]{2,0,1:T(4,128)}), f32[3,256,512]{2,0,1:T(4,128)}, u32[]{:S(2)}, u32[]{:S(2)}) async-start(f32[3,256,512]{2,0,1:T(4,128)} %bitcast.1), calls=%async_computation | async-start | bytes 4194304 | tf_op jit(solution)/shard_map/all_to_all | solution.py:79
  44.1 10.4 %fusion = f32[512,6,256,1]{0,2,3,1:T(8,128)S(1)} fusion(f32[3,1,256,6,1,256]{5,4,3,2,1,0:T(1,128)} %param.7, f32[3,256,512]{2,0,1:T(4,128)S(1)} %all-to-all-done.2), kind=kOutput, calls=%fused_computation | convolution fusion | flops 7247757312 | bytes 9437184 | tf_op jit(solution)/shard_map/lsmt,lsw->mtw/dot_general | solution.py:80
  54.5 2.0 copy.45
  56.6 13.3 %all-to-all-done = f32[3,256,512]{2,0,1:T(4,128)} async-done(((f32[3,256,512]{2,0,1:T(4,128)}), f32[3,256,512]{2,0,1:T(4,128)}, u32[]{:S(2)}, u32[]{:S(2)}) %all-to-all-start) | async-done | bytes 1572896 | tf_op jit(solution)/shard_map/all_to_all | solution.py:79
  69.9 7.4 %all-to-all-start.3 = ((f32[3,16,32,512]{3,2,0,1:T(8,128)}), f32[3,16,32,512]{3,2,0,1:T(8,128)S(1)}, u32[]{:S(2)}, u32[]{:S(2)}) async-start(f32[3,16,32,512]{3,2,0,1:T(8,128)} %copy.45), calls=%async_computation.3 | async-start | bytes 6291456 | tf_op jit(solution)/shard_map/all_to_all | solution.py:88
  77.4 11.0 %fusion.2 = f32[512,6,256,1]{0,2,3,1:T(8,128)S(1)} fusion(f32[3,1,256,6,1,256]{5,4,3,2,1,0:T(1,128)} %param.7, f32[3,256,512]{2,0,1:T(4,128)} %all-to-all-done), kind=kOutput, calls=%fused_computation.2 | convolution fusion | flops 7247757312 | bytes 9437184 | tf_op jit(solution)/shard_map/lsmt,lsw->mtw/dot_general | solution.py:80
  88.4 2.1 copy.41
  90.5 24.7 %all-to-all-done.3 = f32[3,16,32,512]{3,2,0,1:T(8,128)S(1)} async-done(((f32[3,16,32,512]{3,2,0,1:T(8,128)}), f32[3,16,32,512]{3,2,0,1:T(8,128)S(1)}, u32[]{:S(2)}, u32[]{:S(2)}) %all-to-all-start.3) | async-done | bytes 3145760 | tf_op jit(solution)/shard_map/all_to_all | solution.py:88
  115.2 7.0 %all-to-all-start.1 = ((f32[3,16,32,512]{3,2,0,1:T(8,128)}), f32[3,16,32,512]{3,2,0,1:T(8,128)}, u32[]{:S(2)}, u32[]{:S(2)}) async-start(f32[3,16,32,512]{3,2,0,1:T(8,128)} %copy.41), calls=%async_computation.1 | async-start | bytes 6291456 | tf_op jit(solution)/shard_map/all_to_all | solution.py:88
  123.1 4.5 %collective-permute-start.1 = (f32[3,32,1024]{2,1,0:T(8,128)}, f32[3,32,1024]{2,1,0:T(8,128)}, u32[]{:S(2)}, u32[]{:S(2)}) collective-permute-start(f32[3,32,1024]{2,1,0:T(8,128)} %pad_maximum_fusion.2), channel_id=1, source_target_pairs={{0,0},{1,8},{2,16},{3,24},{4,32},{5,40},{6,48},{7,56},{8,1},{9,9},... | collective-permute-start | bytes 1179656 | tf_op jit(solution)/shard_map/ppermute | solution.py:71
  128.0 32.2 %all-to-all-done.1 = f32[3,16,32,512]{3,2,0,1:T(8,128)} async-done(((f32[3,16,32,512]{3,2,0,1:T(8,128)}), f32[3,16,32,512]{3,2,0,1:T(8,128)}, u32[]{:S(2)}, u32[]{:S(2)}) %all-to-all-start.1) | async-done | bytes 3145760 | tf_op jit(solution)/shard_map/all_to_all | solution.py:88
  160.2 2.2 reduce_sum.27
  162.5 14.3 %collective-permute-done.1 = f32[3,32,1024]{2,1,0:T(8,128)} collective-permute-done((f32[3,32,1024]{2,1,0:T(8,128)}, f32[3,32,1024]{2,1,0:T(8,128)}, u32[]{:S(2)}, u32[]{:S(2)}) %collective-permute-start.1) | collective-permute-done | bytes 393248 | tf_op jit(solution)/shard_map/ppermute | solution.py:71
  176.8 2.0 convolution_bitcast_fusion
  178.8 2.0 convolution_bitcast_fusion.1
  181.1 26.9 %all_to_all.35 = f32[128,1,2560]{2,1,0:T(1,128)S(1)} all-to-all(f32[128,1,2560]{2,1,0:T(1,128)S(1)} %bitcast.151), channel_id=1, replica_groups=mesh['prow'=16,'pcol'=8] {'prow','pcol'}, dimensions={0} | all-to-all | bytes 2621440 | tf_op jit(solution)/shard_map/all_to_all | solution.py:128
  208.8 1.7 broadcast_in_dim.38
  210.5 7.0 %all-to-all-start.5 = ((f32[128,1,2560]{2,1,0:T(1,128)}), f32[128,1,2560]{2,1,0:T(1,128)S(1)}, u32[]{:S(2)}, u32[]{:S(2)}) async-start(f32[128,1,2560]{2,1,0:T(1,128)} %broadcast_in_dim.38), calls=%async_computation.5 | async-start | bytes 2621440 | tf_op jit(solution)/shard_map/all_to_all | solution.py:130
  217.5 6.3 %collective-permute-start = (f32[3,32,1024]{2,1,0:T(8,128)S(1)}, f32[3,32,1024]{2,1,0:T(8,128)S(1)}, u32[]{:S(2)}, u32[]{:S(2)}) collective-permute-start(f32[3,32,1024]{2,1,0:T(8,128)S(1)} %pad_maximum_fusion.1), channel_id=1, source_target_pairs={{0,0},{8,1},{16,2},{24,3},{32,4},{40,5},{48,6},{56,7},{1,8},{9,9},... | collective-permute-start | bytes 1179656 | tf_op jit(solution)/shard_map/ppermute | solution.py:124
  223.9 29.8 %collective-permute-done = f32[3,32,1024]{2,1,0:T(8,128)S(1)} collective-permute-done((f32[3,32,1024]{2,1,0:T(8,128)S(1)}, f32[3,32,1024]{2,1,0:T(8,128)S(1)}, u32[]{:S(2)}, u32[]{:S(2)}) %collective-permute-start) | collective-permute-done | bytes 393248 | tf_op jit(solution)/shard_map/ppermute | solution.py:124
  257.1 1.8 fusion.10
  (47 shorter events, 10.6 us)
Async XLA Ops:
  5.2 6.9 %copy-start.3 = (f32[3,1,32,512]{3,2,1,0:T(8,128)S(1)}, f32[3,1,32,512]{3,2,1,0:T(8,128)}, u32[]{:S(2)}) copy-start(f32[3,1,32,512]{3,2,1,0:T(8,128)} %param.8) | copy-start | bytes 589828
  5.2 32.4 %all-to-all-start.2 = ((f32[3,256,512]{2,0,1:T(4,128)}), f32[3,256,512]{2,0,1:T(4,128)S(1)}, u32[]{:S(2)}, u32[]{:S(2)}) async-start(f32[3,256,512]{2,0,1:T(4,128)} %bitcast.11), calls=%async_computation.2 | async-start | bytes 4194304 | tf_op jit(solution)/shard_map/all_to_all | solution.py:79
  39.3 30.6 %all-to-all-start = ((f32[3,256,512]{2,0,1:T(4,128)}), f32[3,256,512]{2,0,1:T(4,128)}, u32[]{:S(2)}, u32[]{:S(2)}) async-start(f32[3,256,512]{2,0,1:T(4,128)} %bitcast.1), calls=%async_computation | async-start | bytes 4194304 | tf_op jit(solution)/shard_map/all_to_all | solution.py:79
  69.9 45.3 %all-to-all-start.3 = ((f32[3,16,32,512]{3,2,0,1:T(8,128)}), f32[3,16,32,512]{3,2,0,1:T(8,128)S(1)}, u32[]{:S(2)}, u32[]{:S(2)}) async-start(f32[3,16,32,512]{3,2,0,1:T(8,128)} %copy.45), calls=%async_computation.3 | async-start | bytes 6291456 | tf_op jit(solution)/shard_map/all_to_all | solution.py:88
  90.5 31.7 %copy-start.2 = (f32[3,1,32,512]{3,2,1,0:T(8,128)S(1)}, f32[3,1,32,512]{3,2,1,0:T(8,128)}, u32[]{:S(2)}) copy-start(f32[3,1,32,512]{3,2,1,0:T(8,128)} %param.9) | copy-start | bytes 589828
  115.2 45.0 %all-to-all-start.1 = ((f32[3,16,32,512]{3,2,0,1:T(8,128)}), f32[3,16,32,512]{3,2,0,1:T(8,128)}, u32[]{:S(2)}, u32[]{:S(2)}) async-start(f32[3,16,32,512]{3,2,0,1:T(8,128)} %copy.41), calls=%async_computation.1 | async-start | bytes 6291456 | tf_op jit(solution)/shard_map/all_to_all | solution.py:88
  123.1 53.7 %collective-permute-start.1 = (f32[3,32,1024]{2,1,0:T(8,128)}, f32[3,32,1024]{2,1,0:T(8,128)}, u32[]{:S(2)}, u32[]{:S(2)}) collective-permute-start(f32[3,32,1024]{2,1,0:T(8,128)} %pad_maximum_fusion.2), channel_id=1, source_target_pairs={{0,0},{1,8},{2,16},{3,24},{4,32},{5,40},{6,48},{7,56},{8,1},{9,9},... | collective-permute-start | bytes 1179656 | tf_op jit(solution)/shard_map/ppermute | solution.py:71
  210.5 43.9 %all-to-all-start.5 = ((f32[128,1,2560]{2,1,0:T(1,128)}), f32[128,1,2560]{2,1,0:T(1,128)S(1)}, u32[]{:S(2)}, u32[]{:S(2)}) async-start(f32[128,1,2560]{2,1,0:T(1,128)} %broadcast_in_dim.38), calls=%async_computation.5 | async-start | bytes 2621440 | tf_op jit(solution)/shard_map/all_to_all | solution.py:130
  217.5 36.1 %collective-permute-start = (f32[3,32,1024]{2,1,0:T(8,128)S(1)}, f32[3,32,1024]{2,1,0:T(8,128)S(1)}, u32[]{:S(2)}, u32[]{:S(2)}) collective-permute-start(f32[3,32,1024]{2,1,0:T(8,128)S(1)} %pad_maximum_fusion.1), channel_id=1, source_target_pairs={{0,0},{8,1},{16,2},{24,3},{32,4},{40,5},{48,6},{56,7},{1,8},{9,9},... | collective-permute-start | bytes 1179656 | tf_op jit(solution)/shard_map/ppermute | solution.py:124
  255.5 1.2 copy-start
  255.5 1.5 copy-start.1

commit v4 on v3

--- a/solution.py
+++ b/solution.py
@@ -33,10 +33,13 @@
 def body(
     inverse_block, panel_first, panel_second, diag_first, diag_second, pattern_first, pattern_second
 ):
-    row_count = lax.axis_size("prow")
+    prow = ("prow_hi", "core")
+    row_count = lax.axis_size(prow)
+    pair = lax.axis_size("core")
+    core = lax.axis_index("core")
     col_count = lax.axis_size("pcol")
     factor = row_count // col_count
-    row_index = lax.axis_index("prow")
+    row_index = lax.axis_index(prow)
     col_index = lax.axis_index("pcol")
     row_blocks = inverse_block.shape[0]
     block_rows = inverse_block.shape[2]
@@ -44,7 +47,14 @@
     slice_rows = panel_first.shape[2]
     width = panel_first.shape[3]
     highest = lax.Precision.HIGHEST
-    both = ("prow", "pcol")
+    both = ("prow_hi", "core", "pcol")
+    swap = [(b, (b + 1) % pair) for b in range(pair)]
+
+    def pair_sum(value, axis):
+        split = value.reshape(value.shape[:axis] + (value.shape[axis] // pair, pair) + value.shape[axis + 1:])
+        mine = lax.dynamic_index_in_dim(split, core, axis + 1, False)
+        other = lax.dynamic_index_in_dim(split, (core + 1) % pair, axis + 1, False)
+        return mine + lax.ppermute(other, "core", swap)
 
     def kept_of(pattern, prow):
         return lax.dynamic_index_in_dim(
@@ -85,7 +95,7 @@
             preferred_element_type=jnp.float32,
         )
         chunks = partial.reshape(row_blocks, row_count, slice_rows, piece.shape[-1])
-        received = lax.all_to_all(chunks, "prow", 1, 1, tiled=True)
+        received = lax.all_to_all(pair_sum(chunks, 1), "prow_hi", 1, 1, tiled=True)
         return jnp.sum(received, axis=1)
 
     total = jnp.concatenate(
@@ -122,12 +132,20 @@
         ]
     )
     column_home = lax.ppermute(column, both, to_owner)
-    devices = row_count * col_count
     packed = pack_upper(parts)
-    flat = packed.reshape(devices, packed.size // devices)
-    reduced = jnp.sum(lax.all_to_all(flat, both, 0, 0, tiled=True), axis=0)
+    others = ("prow_hi", "pcol")
+    devices = lax.axis_size(others)
+    half = pair_sum(packed.reshape(pair * devices, packed.size // (pair * devices)), 0)
+    flat = half.reshape(devices, half.size // devices)
+    reduced = jnp.sum(lax.all_to_all(flat, others, 0, 0, tiled=True), axis=0)
     spread_sum = jnp.broadcast_to(reduced[None], flat.shape)
-    summed = lax.all_to_all(spread_sum, both, 0, 0, tiled=True).reshape(packed.shape)
+    mine = lax.all_to_all(spread_sum, others, 0, 0, tiled=True).reshape(half.shape)
+    other = lax.ppermute(mine, "core", swap)
+    summed = jnp.where(
+        core == 0,
+        jnp.stack([mine, other], axis=1),
+        jnp.stack([other, mine], axis=1),
+    ).reshape(packed.shape)
     sums = unpack_upper(summed, width // TILE)
     return (
         column_home[:, None, :, :width],
@@ -138,10 +156,13 @@
 
 
 def solution(mesh):
+    rows, cols = mesh.devices.shape
+    split = jax.sharding.Mesh(mesh.devices.reshape(rows // 2, 2, cols), ("prow_hi", "core", "pcol"))
+    prow = ("prow_hi", "core")
     placed = (
-        P(None, "prow", None, None, "pcol", None),
-        P(None, "prow", "pcol", None),
-        P(None, "prow", "pcol", None),
+        P(None, prow, None, None, "pcol", None),
+        P(None, prow, "pcol", None),
+        P(None, prow, "pcol", None),
         P(),
         P(),
         P(),
@@ -149,8 +170,8 @@
     )
     return jax.shard_map(
         body,
-        mesh=mesh,
+        mesh=split,
         in_specs=placed,
-        out_specs=(P(None, "prow", "pcol", None), P(None, "prow", "pcol", None), P(), P()),
+        out_specs=(P(None, prow, "pcol", None), P(None, prow, "pcol", None), P(), P()),
         check_vma=False,
     )

time: 260 us -> 240 us (0.923)
  waiting for transfers between devices: 140 us -> 109 us
  blocking collectives: 26.9 us -> 39.2 us
  starting transfers between devices: 44 us -> 35.2 us
  other arithmetic: 7.93 us -> 13.2 us
    all_to_all x3 -> x2, waiting for transfers between devices: 56.9 us -> 32.4 us  [reduce_piece(): received = lax.all_to_all(pair_sum(chunks, 1), 'prow_hi', 1, 1, tiled=True)]
    all_to_all x1 -> x2, blocking collectives: 26.9 us -> 39.2 us  [the longest x1 21.1 us: body(): reduced = jnp.sum(lax.all_to_all(flat, others, 0, 0, tiled=True), axis=0)]
    ppermute x1, waiting for transfers between devices: 29.8 us -> 19.2 us  [body(): column_home = lax.ppermute(column, both, to_owner)]
    all_to_all x3 -> x2, starting transfers between devices: 21.4 us -> 13.6 us  [reduce_piece(): received = lax.all_to_all(pair_sum(chunks, 1), 'prow_hi', 1, 1, tiled=True)]
    add x0 -> x3, other arithmetic: none -> 5.89 us  [pair_sum(): return mine + lax.ppermute(other, 'core', swap)]
    dynamic_slice x0 -> x5, local copies, waits for them, and re-layouts: none -> 4.33 us  [the longest x2 2.56 us: pair_sum(): other = lax.dynamic_index_in_dim(split, (core + 1) % pair, axis + 1, False)]
    reshape x2 -> x0, local copies, waits for them, and re-layouts: 4.11 us -> none  [reduce_piece(): chunks = partial.reshape(row_blocks, row_count, slice_rows, piece.shape[-1])]
  transfers between devices with their start and end apart: 7 -> 10, of which waited for: 6 -> 7; matrix products, arithmetic and copies ran while one was open for 12% -> 14% of each run, Pallas kernels for 0% -> 0%
where the time goes in v4:
time: 240 us; the launch traced here: 239 us
  waiting for transfers between devices  109 us (45%)
  blocking collectives  39.2 us (16%)
  starting transfers between devices  35.2 us (15%)
  matrix products  25.3 us (11%)
  local copies, waits for them, and re-layouts  15.7 us (7%)
  other arithmetic  13.2 us (6%)
    all_to_all x2, waiting for transfers between devices, reduce_piece(): gathered = lax.all_to_all(spread, 'pcol', 1, 1, tiled=True)  39 us
    all_to_all x2, waiting for transfers between devices, reduce_piece(): received = lax.all_to_all(pair_sum(chunks, 1), 'prow_hi', 1, 1, tiled=True)  32.4 us
    dot_general x2, matrix products, reduce_piece(): jnp.einsum('lsmt,lsw->mtw', matrix, gathered, precision=highest, preferre...  21.4 us
    all_to_all x1, blocking collectives, body(): reduced = jnp.sum(lax.all_to_all(flat, others, 0, 0, tiled=True), axis=0)  21.1 us
    ppermute x1, waiting for transfers between devices, body(): column_home = lax.ppermute(column, both, to_owner)  19.2 us
    all_to_all x1, blocking collectives, body(): lax.all_to_all(spread_sum, others, 0, 0, tiled=True).reshape(half.shape)  18.1 us
    ppermute x1, waiting for transfers between devices, body(): x_at_reducer = lax.ppermute(x, both, to_reducer)  16.4 us
    all_to_all x2, starting transfers between devices, reduce_piece(): received = lax.all_to_all(pair_sum(chunks, 1), 'prow_hi', 1, 1, tiled=True)  13.6 us
  transfers between devices with their start and end apart: 10, of which 7 were waited for; matrix products, arithmetic and copies ran while one was open for 14% of the time, Pallas kernels for 0%

profile of v4, /device:TPU:6, one launch (start us, length us, event | category | flops | bytes accessed | tf_op | source)
XLA Modules:
  0.0 238.7 jit_solution(1672642961132354922)
XLA Ops:
  5.2 6.9 %all-to-all-start.2 = ((f32[3,256,512]{2,0,1:T(4,128)}), f32[3,256,512]{2,0,1:T(4,128)S(1)}, u32[]{:S(2)}, u32[]{:S(2)}) async-start(f32[3,256,512]{2,0,1:T(4,128)} %bitcast.15), calls=%async_computation.2 | async-start | bytes 4194304 | tf_op jit(solution)/shard_map/all_to_all | solution.py:89
  12.3 25.2 %all-to-all-done.2 = f32[3,256,512]{2,0,1:T(4,128)S(1)} async-done(((f32[3,256,512]{2,0,1:T(4,128)}), f32[3,256,512]{2,0,1:T(4,128)S(1)}, u32[]{:S(2)}, u32[]{:S(2)}) %all-to-all-start.2) | async-done | bytes 1572896 | tf_op jit(solution)/shard_map/all_to_all | solution.py:89
  37.6 1.7 broadcast_in_dim.15
  39.3 4.8 %all-to-all-start = ((f32[3,256,512]{2,0,1:T(4,128)}), f32[3,256,512]{2,0,1:T(4,128)}, u32[]{:S(2)}, u32[]{:S(2)}) async-start(f32[3,256,512]{2,0,1:T(4,128)} %bitcast.1), calls=%async_computation | async-start | bytes 4194304 | tf_op jit(solution)/shard_map/all_to_all | solution.py:89
  44.1 10.4 %fusion = f32[512,6,256,1]{0,2,3,1:T(8,128)S(1)} fusion(f32[3,1,256,6,1,256]{5,4,3,2,1,0:T(1,128)} %param.7, f32[3,256,512]{2,0,1:T(4,128)S(1)} %all-to-all-done.2), kind=kOutput, calls=%fused_computation | convolution fusion | flops 7247757312 | bytes 9437184 | tf_op jit(solution)/shard_map/lsmt,lsw->mtw/dot_general | solution.py:90
  56.1 13.8 %all-to-all-done = f32[3,256,512]{2,0,1:T(4,128)} async-done(((f32[3,256,512]{2,0,1:T(4,128)}), f32[3,256,512]{2,0,1:T(4,128)}, u32[]{:S(2)}, u32[]{:S(2)}) %all-to-all-start) | async-done | bytes 1572896 | tf_op jit(solution)/shard_map/all_to_all | solution.py:89
  69.9 11.0 %fusion.2 = f32[512,6,256,1]{0,2,3,1:T(8,128)S(1)} fusion(f32[3,1,256,6,1,256]{5,4,3,2,1,0:T(1,128)} %param.7, f32[3,256,512]{2,0,1:T(4,128)} %all-to-all-done), kind=kOutput, calls=%fused_computation.2 | convolution fusion | flops 7247757312 | bytes 9437184 | tf_op jit(solution)/shard_map/lsmt,lsw->mtw/dot_general | solution.py:90
  82.5 2.9 %bitcast_add_fusion = f32[3,8,32,512]{3,2,0,1:T(8,128)} fusion(f32[3,8,32,512]{3,2,0,1:T(8,128)} %collective-permute-done.1, f32[3,8,1,32,512]{4,3,2,1,0:T(8,128)S(1)} %get-tuple-element.10), kind=kLoop, calls=%fused_computation.7 | loop fusion | flops 393216 | bytes 4718592 | tf_op jit(solution)/shard_map/add | solution.py:57
  85.4 7.4 %all-to-all-start.3 = ((f32[3,8,32,512]{3,2,0,1:T(8,128)}), f32[3,8,32,512]{3,2,0,1:T(8,128)S(1)}, u32[]{:S(2)}, u32[]{:S(2)}) async-start(f32[3,8,32,512]{3,2,0,1:T(8,128)} %bitcast_add_fusion), calls=%async_computation.3 | async-start | bytes 3145728 | tf_op jit(solution)/shard_map/all_to_all | solution.py:98
  92.9 2.9 %bitcast_add_fusion.1 = f32[3,8,32,512]{3,2,0,1:T(8,128)} fusion(f32[3,8,32,512]{3,2,0,1:T(8,128)} %collective-permute-done, f32[3,8,1,32,512]{4,3,2,1,0:T(8,128)S(1)} %get-tuple-element.8), kind=kLoop, calls=%fused_computation.9 | loop fusion | flops 393216 | bytes 4718592 | tf_op jit(solution)/shard_map/add | solution.py:57
  95.8 17.9 %all-to-all-done.3 = f32[3,8,32,512]{3,2,0,1:T(8,128)S(1)} async-done(((f32[3,8,32,512]{3,2,0,1:T(8,128)}), f32[3,8,32,512]{3,2,0,1:T(8,128)S(1)}, u32[]{:S(2)}, u32[]{:S(2)}) %all-to-all-start.3) | async-done | bytes 1572896 | tf_op jit(solution)/shard_map/all_to_all | solution.py:98
  113.7 6.2 %all-to-all-start.1 = ((f32[3,8,32,512]{3,2,0,1:T(8,128)}), f32[3,8,32,512]{3,2,0,1:T(8,128)S(1)}, u32[]{:S(2)}, u32[]{:S(2)}) async-start(f32[3,8,32,512]{3,2,0,1:T(8,128)} %bitcast_add_fusion.1), calls=%async_computation.1 | async-start | bytes 3145728 | tf_op jit(solution)/shard_map/all_to_all | solution.py:98
  120.9 4.3 %collective-permute-start.3 = (f32[3,32,1024]{2,1,0:T(8,128)}, f32[3,32,1024]{2,1,0:T(8,128)}, u32[]{:S(2)}, u32[]{:S(2)}) collective-permute-start(f32[3,32,1024]{2,1,0:T(8,128)} %pad_maximum_fusion.2), channel_id=1, source_target_pairs={{0,0},{1,8},{2,16},{3,24},{4,32},{5,40},{6,48},{7,56},{8,1},{9,9},... | collective-permute-start | bytes 1179656 | tf_op jit(solution)/shard_map/ppermute | solution.py:81
  125.3 14.5 %all-to-all-done.1 = f32[3,8,32,512]{3,2,0,1:T(8,128)S(1)} async-done(((f32[3,8,32,512]{3,2,0,1:T(8,128)}), f32[3,8,32,512]{3,2,0,1:T(8,128)S(1)}, u32[]{:S(2)}, u32[]{:S(2)}) %all-to-all-start.1) | async-done | bytes 1572896 | tf_op jit(solution)/shard_map/all_to_all | solution.py:98
  140.2 16.4 %collective-permute-done.3 = f32[3,32,1024]{2,1,0:T(8,128)} collective-permute-done((f32[3,32,1024]{2,1,0:T(8,128)}, f32[3,32,1024]{2,1,0:T(8,128)}, u32[]{:S(2)}, u32[]{:S(2)}) %collective-permute-start.3) | collective-permute-done | bytes 393248 | tf_op jit(solution)/shard_map/ppermute | solution.py:81
  156.5 2.0 convolution_bitcast_fusion
  158.5 2.0 convolution_bitcast_fusion.1
  162.8 2.1 collective-permute-done.4
  165.5 21.1 %all_to_all.38 = f32[64,1,2560]{2,1,0:T(1,128)S(1)} all-to-all(f32[64,1,2560]{2,1,0:T(1,128)S(1)} %all_to_all.28), channel_id=1, replica_groups=mesh['prow_hi'=8,'core'=2,'pcol'=8] {'prow_hi','pcol'}, dimensions={0} | all-to-all | bytes 1310720 | tf_op jit(solution)/shard_map/all_to_all | solution.py:140
  187.3 18.1 %all_to_all.39 = f32[64,1,2560]{2,1,0:T(1,128)S(1)} all-to-all(f32[64,1,2560]{2,1,0:T(1,128)S(1)} %broadcast_in_dim.38), channel_id=1, replica_groups=mesh['prow_hi'=8,'core'=2,'pcol'=8] {'prow_hi','pcol'}, dimensions={0} | all-to-all | bytes 1310720 | tf_op jit(solution)/shard_map/all_to_all | solution.py:142
  205.6 5.3 %collective-permute-start.2 = (f32[3,32,1024]{2,1,0:T(8,128)S(1)}, f32[3,32,1024]{2,1,0:T(8,128)S(1)}, u32[]{:S(2)}, u32[]{:S(2)}) collective-permute-start(f32[3,32,1024]{2,1,0:T(8,128)S(1)} %pad_maximum_fusion.1), channel_id=1, source_target_pairs={{0,0},{8,1},{16,2},{24,3},{32,4},{40,5},{48,6},{56,7},{1,8},{9,9},... | collective-permute-start | bytes 1179656 | tf_op jit(solution)/shard_map/ppermute | solution.py:134
  210.9 19.2 %collective-permute-done.2 = f32[3,32,1024]{2,1,0:T(8,128)S(1)} collective-permute-done((f32[3,32,1024]{2,1,0:T(8,128)S(1)}, f32[3,32,1024]{2,1,0:T(8,128)S(1)}, u32[]{:S(2)}, u32[]{:S(2)}) %collective-permute-start.2) | collective-permute-done | bytes 393248 | tf_op jit(solution)/shard_map/ppermute | solution.py:134
  231.3 1.9 maximum_select_fusion
  236.9 1.8 fusion.10
  (67 shorter events, 17.8 us)
Async XLA Ops:
  5.2 6.9 %copy-start.3 = (f32[3,1,32,512]{3,2,1,0:T(8,128)S(1)}, f32[3,1,32,512]{3,2,1,0:T(8,128)}, u32[]{:S(2)}) copy-start(f32[3,1,32,512]{3,2,1,0:T(8,128)} %param.8) | copy-start | bytes 589828
  5.2 32.4 %all-to-all-start.2 = ((f32[3,256,512]{2,0,1:T(4,128)}), f32[3,256,512]{2,0,1:T(4,128)S(1)}, u32[]{:S(2)}, u32[]{:S(2)}) async-start(f32[3,256,512]{2,0,1:T(4,128)} %bitcast.15), calls=%async_computation.2 | async-start | bytes 4194304 | tf_op jit(solution)/shard_map/all_to_all | solution.py:89
  39.3 30.6 %all-to-all-start = ((f32[3,256,512]{2,0,1:T(4,128)}), f32[3,256,512]{2,0,1:T(4,128)}, u32[]{:S(2)}, u32[]{:S(2)}) async-start(f32[3,256,512]{2,0,1:T(4,128)} %bitcast.1), calls=%async_computation | async-start | bytes 4194304 | tf_op jit(solution)/shard_map/all_to_all | solution.py:89
  56.1 26.4 %collective-permute-start.1 = (f32[3,8,32,512]{3,2,0,1:T(8,128)}, f32[3,8,32,512]{3,2,0,1:T(8,128)}, u32[]{:S(2)}, u32[]{:S(2)}) collective-permute-start(f32[3,8,32,512]{3,2,0,1:T(8,128)} %bitcast.162), channel_id=1, source_target_pairs={{0,8},{8,0},{1,9},{9,1},{2,10},{10,2},{3,11},{11,3},{4,12},{12,4},... | collective-permute-start | bytes 4718600 | tf_op jit(solution)/shard_map/ppermute | solution.py:57
  82.5 10.3 %collective-permute-start = (f32[3,8,32,512]{3,2,0,1:T(8,128)}, f32[3,8,32,512]{3,2,0,1:T(8,128)}, u32[]{:S(2)}, u32[]{:S(2)}) collective-permute-start(f32[3,8,32,512]{3,2,0,1:T(8,128)} %bitcast.163), channel_id=1, source_target_pairs={{0,8},{8,0},{1,9},{9,1},{2,10},{10,2},{3,11},{11,3},{4,12},{12,4},... | collective-permute-start | bytes 4718600 | tf_op jit(solution)/shard_map/ppermute | solution.py:57
  85.4 28.3 %all-to-all-start.3 = ((f32[3,8,32,512]{3,2,0,1:T(8,128)}), f32[3,8,32,512]{3,2,0,1:T(8,128)S(1)}, u32[]{:S(2)}, u32[]{:S(2)}) async-start(f32[3,8,32,512]{3,2,0,1:T(8,128)} %bitcast_add_fusion), calls=%async_computation.3 | async-start | bytes 3145728 | tf_op jit(solution)/shard_map/all_to_all | solution.py:98
  95.8 24.1 %copy-start.2 = (f32[3,1,32,512]{3,2,1,0:T(8,128)S(1)}, f32[3,1,32,512]{3,2,1,0:T(8,128)}, u32[]{:S(2)}) copy-start(f32[3,1,32,512]{3,2,1,0:T(8,128)} %param.9) | copy-start | bytes 589828
  113.7 26.1 %all-to-all-start.1 = ((f32[3,8,32,512]{3,2,0,1:T(8,128)}), f32[3,8,32,512]{3,2,0,1:T(8,128)S(1)}, u32[]{:S(2)}, u32[]{:S(2)}) async-start(f32[3,8,32,512]{3,2,0,1:T(8,128)} %bitcast_add_fusion.1), calls=%async_computation.1 | async-start | bytes 3145728 | tf_op jit(solution)/shard_map/all_to_all | solution.py:98
  120.9 35.7 %collective-permute-start.3 = (f32[3,32,1024]{2,1,0:T(8,128)}, f32[3,32,1024]{2,1,0:T(8,128)}, u32[]{:S(2)}, u32[]{:S(2)}) collective-permute-start(f32[3,32,1024]{2,1,0:T(8,128)} %pad_maximum_fusion.2), channel_id=1, source_target_pairs={{0,0},{1,8},{2,16},{3,24},{4,32},{5,40},{6,48},{7,56},{8,1},{9,9},... | collective-permute-start | bytes 1179656 | tf_op jit(solution)/shard_map/ppermute | solution.py:81
  162.7 2.2 collective-permute-start.4
  205.4 25.4 %collective-permute-start.5 = (f32[64,2560]{1,0:T(8,128)S(1)}, f32[64,2560]{1,0:T(8,128)S(1)}, u32[]{:S(2)}, u32[]{:S(2)}) collective-permute-start(f32[64,2560]{1,0:T(8,128)S(1)} %bitcast.172), channel_id=1, source_target_pairs={{0,8},{8,0},{1,9},{9,1},{2,10},{10,2},{3,11},{11,3},{4,12},{12,4},... | collective-permute-start | bytes 1966088 | tf_op jit(solution)/shard_map/ppermute | solution.py:143
  205.6 24.5 %collective-permute-start.2 = (f32[3,32,1024]{2,1,0:T(8,128)S(1)}, f32[3,32,1024]{2,1,0:T(8,128)S(1)}, u32[]{:S(2)}, u32[]{:S(2)}) collective-permute-start(f32[3,32,1024]{2,1,0:T(8,128)S(1)} %pad_maximum_fusion.1), channel_id=1, source_target_pairs={{0,0},{8,1},{16,2},{24,3},{32,4},{40,5},{48,6},{56,7},{1,8},{9,9},... | collective-permute-start | bytes 1179656 | tf_op jit(solution)/shard_map/ppermute | solution.py:134
  235.4 1.2 copy-start
  235.4 1.5 copy-start.1
